TPU v7x, 128 devices: a whole 4x4x4 slice. The times are simulated.
128 devices in a mesh: row: 16 (over z_lo, x, core), col: 8 (over y, z_hi).
Axes of the slice: x: 4, y: 4, z: 4 (z_hi: 2, z_lo: 2; z = z_hi * 2 + z_lo), core: 2. Of those that a mesh axis runs over, the one named last changes fastest.
Arguments:
- slab_embed: float32 [65536, 768], P(('col', 'row')), may hold values from -1 to 1
- coverage_old: float32 [65536], P('col'), may hold values from 2 to 4.5
- sel_index: int32 [2048], P('row'), may hold values from 0 to 65535
- cand_index: int32 [3072], P('row'), may hold values from 0 to 65535
Outputs:
- coverage: float32 [65536], P('col')
- total_gain: float32 [3072], P('row')
Inputs may be any that keep to these rules, and one draw needn't show every extreme that they name: `sel_index`: indices into the slab. `cand_index`: indices into the slab.
All inputs are finite; a program needn't handle non-finite values.
Results may differ from a plain program's by a relative error of at most 0.00014.
Values sent between devices are 32-bit elements; how exact they have to be, the bound alone decides.
No kernel may reach another device: no remote copies, remote signals or barrier semaphores. Data moves between devices by JAX's collectives and lax.ppermute only.
A program may use at most 128 MiB of HBM per device.

v0:
```python
import jax
import jax.numpy as jnp
from jax import lax
from jax.sharding import Mesh
from jax.sharding import PartitionSpec as P

N_Y, N_Z = (4, 2)


def similar(left, right):
    return lax.dot_general(
        left,
        right,
        (((1,), (1,)), ((), ())),
        precision=lax.Precision.HIGH,
        preferred_element_type=jnp.float32,
    )


def lookup(source, indices, first_row):
    position = indices - first_row
    inside = (position >= 0) & (position < source.shape[0])
    picked = jnp.take(source, jnp.clip(position, 0, source.shape[0] - 1), axis=0)
    return jnp.where(inside[:, None], picked, 0.0)


def col_of(y, z):
    return y % N_Y * N_Z + z


def y_shift(value, step):
    pairs = [(col_of(y, z), col_of(y + step, z)) for y in range(N_Y) for z in range(N_Z)]
    return lax.ppermute(value, "col", pairs)


def pair_split(value, low):
    halves = value.reshape(2, value.shape[0] // 2, *value.shape[1:])
    return (jnp.where(low, halves[0], halves[1]), jnp.where(low, halves[1], halves[0]))


def pair_join(mine, other, low):
    return jnp.where(low, jnp.concatenate([mine, other]), jnp.concatenate([other, mine]))


def z_group_shift(value, k):
    if k == 1:
        return lax.ppermute(value, "col", [(c, c ^ 1) for c in range(N_Y * N_Z)])
    if k == 2:
        return lax.ppermute(value, "zl", [(0, 1), (1, 0)])
    n = 2 * N_Y * N_Z
    return lax.ppermute(value, ("zl", "col"), [(i, i ^ N_Y * N_Z ^ 1) for i in range(n)])


def group_masked_sum(value):
    here = lax.axis_index("col")
    y, z = (here // N_Z, here % N_Z)
    g = lax.axis_index("zl") * 2 + z
    quarter = value.shape[0] // N_Y

    def part(k):
        return lax.dynamic_slice_in_dim(value, (y + k) % N_Y * quarter, quarter)

    own = part(0)
    for k in range(1, N_Y):
        own = own + y_shift(part(k), k)
    piece = quarter // 4

    def z_part(k):
        return lax.dynamic_slice_in_dim(own, (g ^ k) * piece, piece)

    mine = z_part(0)
    for k in range(1, 4):
        mine = mine + z_group_shift(z_part(k), k)
    received = jnp.stack([mine] + [z_group_shift(mine, k) for k in range(1, 4)])
    own = jnp.take(received, jnp.arange(4) ^ g, axis=0).reshape(own.shape)
    pieces = [own] + [y_shift(own, -k) for k in range(1, N_Y)]
    return jnp.roll(jnp.stack(pieces), y, axis=0).reshape(value.shape)


def all_max_two_rounds(value, axis, n):
    for bits in ((1, 2, 3), (4,)):
        received = [lax.ppermute(value, axis, [(i, i ^ k) for i in range(n)]) for k in bits]
        for other in received:
            value = jnp.maximum(value, other)
    return value


def group_sum_in_order(value):
    here = lax.axis_index("col")
    y, z = (here // N_Z, here % N_Z)
    g = lax.axis_index("zl") * 2 + z
    received = jnp.stack([value] + [z_group_shift(value, k) for k in range(1, 4)])
    z_sum = jnp.sum(jnp.take(received, jnp.arange(4) ^ g, axis=0), axis=0)
    col_pairs = [[(c, c ^ 2 * k) for c in range(N_Y * N_Z)] for k in range(1, N_Y)]
    received = jnp.stack([z_sum] + [lax.ppermute(z_sum, "col", pairs) for pairs in col_pairs])
    return jnp.sum(jnp.take(received, jnp.arange(N_Y) ^ y, axis=0), axis=0)


def all_max(value, axis, n):
    bit = 1
    while bit < n:
        value = jnp.maximum(value, lax.ppermute(value, axis, [(i, i ^ bit) for i in range(n)]))
        bit *= 2
    return value


def gather_in_order(parts, axis, n):
    here = lax.axis_index(axis)
    bit = 1
    while bit < n:
        other = lax.ppermute(parts, axis, [(i, i ^ bit) for i in range(n)])
        low = here & bit == 0
        parts = jnp.where(low, jnp.concatenate([parts, other]), jnp.concatenate([other, parts]))
        bit *= 2
    return parts


def body(slab_embed, coverage_old, sel_index, cand_index):
    n_xc = 8
    col_id = lax.axis_index("col")
    zl = lax.axis_index("zl")
    half = lax.all_gather(slab_embed, "xc", axis=0, tiled=True)
    first_row = (col_id * 2 + zl) * half.shape[0]
    zl_swap = [(0, 1), (1, 0)]
    both_sel = pair_join(sel_index, lax.ppermute(sel_index, "zl", zl_swap), zl == 0)
    both_cand = pair_join(cand_index, lax.ppermute(cand_index, "zl", zl_swap), zl == 0)
    selected = group_masked_sum(lookup(half, both_sel, first_row))
    chosen = group_masked_sum(lookup(half, both_cand, first_row))
    n_sel = both_sel.shape[0]
    sel_scores = lax.optimization_barrier(similar(selected, half))
    reached = all_max_two_rounds(jnp.max(sel_scores, axis=0), "xc", n_xc)
    old = lax.dynamic_slice_in_dim(coverage_old, zl * half.shape[0], half.shape[0])
    coverage = jnp.maximum(old, reached)
    gain_part = jnp.sum(jnp.maximum(similar(chosen, half) - coverage[None, :], 0.0), axis=1)
    total = group_sum_in_order(gain_part)
    total_gain = lax.dynamic_slice_in_dim(total, zl * cand_index.shape[0], cand_index.shape[0])
    full_coverage = pair_join(coverage, lax.ppermute(coverage, "zl", zl_swap), zl == 0)
    return (full_coverage, total_gain)


def solution(mesh):
    shape = dict(zip(mesh.axis_names, mesh.devices.shape))
    names, sizes = ([], [])
    for name in mesh.axis_names:
        if name == "row":
            names += ["zl", "xc"]
            sizes += [2, shape["row"] // 2]
        else:
            names.append(name)
            sizes.append(shape[name])
    split = Mesh(mesh.devices.reshape(sizes), tuple(names))
    in_specs = (P(("col", "zl", "xc"), None), P("col"), P(("zl", "xc")), P(("zl", "xc")))
    out_specs = (P("col"), P(("zl", "xc")))
    return jax.shard_map(body, mesh=split, in_specs=in_specs, out_specs=out_specs, check_vma=False)
```

profile of v0, /device:TPU:8, one launch (start us, length us, event | category | flops | bytes accessed | tf_op | source)
XLA Modules:
  0.0 208.8 jit_solution(17445739290626050738)
XLA Ops:
  7.2 0.7 all-gather.2.cloned.1.call-update
  7.9 2.0 collective-permute-start
  10.1 1.4 collective-permute-done
  11.6 1.9 collective-permute-done.18
  14.2 65.1 %all-gather.2.cloned.1.call-done = f32[4096,768]{1,0:T(8,128)} async-done(((f32[512,768]{1,0:T(8,128)}), f32[4096,768]{1,0:T(8,128)}) %all-gather.2.cloned.1.call-update) | async-done | bytes 12582928 | tf_op jit(solution)/shard_map/all_gather | solution.py:122
  79.3 6.0 %gather_fusion = f32[256,768]{1,0:T(8,128)S(1)} fusion(f32[4096,768]{1,0:T(8,128)} %all-gather.2.cloned.1.call-done, s32[1024]{0:T(1024)S(1)} %pad_clamp_fusion.4), kind=kCustom, calls=%fused_computation.2 | custom fusion | bytes 1573888 | tf_op jit(solution)/shard_map/jit(_take)/gather | solution.py:23
  85.5 0.8 constant_dynamic-slice_fusion.13
  86.9 2.4 %collective-permute-start.2 = (f32[64,768]{1,0:T(8,128)}, f32[64,768]{1,0:T(8,128)}, u32[]{:S(2)}, u32[]{:S(2)}) collective-permute-start(f32[64,768]{1,0:T(8,128)} %get-tuple-element.10), channel_id=1, source_target_pairs={{0,4},{1,5},{2,6},{3,7},{4,0},{5,1},{6,2},{7,3},{8,12},{9,13},{10,... | collective-permute-start | bytes 589832 | tf_op jit(solution)/shard_map/ppermute | solution.py:33
  89.3 1.8 collective-permute-start.1
  91.1 7.1 %gather_fusion.2 = f32[384,768]{1,0:T(8,128)S(1)} fusion(f32[4096,768]{1,0:T(8,128)} %all-gather.2.cloned.1.call-done, s32[1024]{0:T(1024)S(1)} %pad_clamp_fusion.2), kind=kCustom, calls=%fused_computation.4 | custom fusion | bytes 2360832 | tf_op jit(solution)/shard_map/jit(_take)/gather | solution.py:23
  98.1 0.9 select_select_fusion
  99.0 0.7 collective-permute-done.1
  99.7 1.1 add_add_fusion.1
  100.8 3.0 %collective-permute-start.6 = (f32[16,768]{1,0:T(8,128)S(1)}, f32[16,768]{1,0:T(8,128)S(1)}, u32[]{:S(2)}, u32[]{:S(2)}) collective-permute-start(f32[16,768]{1,0:T(8,128)S(1)} %get-tuple-element.15), channel_id=1, source_target_pairs={{0,65},{1,64},{2,67},{3,66},{4,69},{5,68},{6,71},{7,70},{64,1},{65... | collective-permute-start | bytes 147464 | tf_op jit(solution)/shard_map/ppermute | solution.py:51
  103.9 2.7 %collective-permute-start.21 = (f32[96,768]{1,0:T(8,128)S(1)}, f32[96,768]{1,0:T(8,128)S(1)}, u32[]{:S(2)}, u32[]{:S(2)}) collective-permute-start(f32[96,768]{1,0:T(8,128)S(1)} %get-tuple-element.6), channel_id=1, source_target_pairs={{0,6},{1,7},{2,0},{3,1},{4,2},{5,3},{6,4},{7,5},{8,14},{9,15},{10,... | collective-permute-start | bytes 884744 | tf_op jit(solution)/shard_map/ppermute | solution.py:33
  106.9 1.9 collective-permute-start.19
  108.9 1.6 collective-permute-start.4
  110.8 2.0 collective-permute-done.5
  112.8 1.7 collective-permute-done.4
  114.5 1.6 collective-permute-start.9
  116.6 2.7 %collective-permute-start.7 = (f32[16,768]{1,0:T(8,128)S(1)}, f32[16,768]{1,0:T(8,128)S(1)}, u32[]{:S(2)}, u32[]{:S(2)}) collective-permute-start(f32[16,768]{1,0:T(8,128)S(1)} %add_add_fusion.3), channel_id=1, source_target_pairs={{0,1},{1,0},{2,3},{3,2},{4,5},{5,4},{6,7},{7,6},{8,9},{9,8},{10,11... | collective-permute-start | bytes 147464 | tf_op jit(solution)/shard_map/ppermute | solution.py:47
  119.8 0.7 collective-permute-done.19
  121.4 4.1 %collective-permute-start.22 = (f32[24,768]{1,0:T(8,128)S(1)}, f32[24,768]{1,0:T(8,128)S(1)}, u32[]{:S(2)}, u32[]{:S(2)}) collective-permute-start(f32[24,768]{1,0:T(8,128)S(1)} %get-tuple-element.11), channel_id=1, source_target_pairs={{0,1},{1,0},{2,3},{3,2},{4,5},{5,4},{6,7},{7,6},{8,9},{9,8},{10,11... | collective-permute-start | bytes 221192 | tf_op jit(solution)/shard_map/ppermute | solution.py:47
  126.1 2.7 %collective-permute-start.10 = (f32[64,768]{1,0:T(8,128)S(1)}, f32[64,768]{1,0:T(8,128)S(1)}, u32[]{:S(2)}, u32[]{:S(2)}) collective-permute-start(f32[64,768]{1,0:T(8,128)S(1)} %bitcast_select_fusion.2), channel_id=1, source_target_pairs={{0,6},{1,7},{2,0},{3,1},{4,2},{5,3},{6,4},{7,5},{8,14},{9,15},{10,... | collective-permute-start | bytes 589832 | tf_op jit(solution)/shard_map/ppermute | solution.py:33
  129.1 1.0 collective-permute-start.27
  130.1 1.3 collective-permute-start.26
  131.4 2.5 %collective-permute-start.25 = (f32[24,768]{1,0:T(8,128)S(1)}, f32[24,768]{1,0:T(8,128)S(1)}, u32[]{:S(2)}, u32[]{:S(2)}) collective-permute-start(f32[24,768]{1,0:T(8,128)S(1)} %add_add_fusion.2), channel_id=1, source_target_pairs={{0,1},{1,0},{2,3},{3,2},{4,5},{5,4},{6,7},{7,6},{8,9},{9,8},{10,11... | collective-permute-start | bytes 221192 | tf_op jit(solution)/shard_map/ppermute | solution.py:47
  134.0 1.3 collective-permute-done.27
  135.3 1.8 collective-permute-start.12
  137.9 3.3 %collective-permute-done.12 = f32[64,768]{1,0:T(8,128)S(1)} collective-permute-done((f32[64,768]{1,0:T(8,128)S(1)}, f32[64,768]{1,0:T(8,128)S(1)}, u32[]{:S(2)}, u32[]{:S(2)}) %collective-permute-start.12) | collective-permute-done | bytes 196640 | tf_op jit(solution)/shard_map/ppermute | solution.py:33
  141.5 10.3 %fusion.13 = f32[256,4096]{1,0:T(8,128)} fusion(f32[256,768]{1,0:T(8,128)S(1)} %bitcast.61, f32[4096,768]{1,0:T(8,128)} %all-gather.2.cloned.1.call-done), kind=kOutput, calls=%fused_computation.86 | convolution fusion | flops 4831838208 | bytes 17563648 | tf_op jit(solution)/shard_map/dot_general | solution.py:11
  151.8 2.4 %reduce_max.9 = f32[4096]{0:T(1024)S(1)} reduce(f32[256,4096]{1,0:T(8,128)} %fusion.13, f32[]{:T(128)} %constant.182.clone.1), dimensions={0}, to_apply=%region_0.1 | reduce | flops 1044480 | bytes 4210692 | tf_op jit(solution)/shard_map/reduce_max | solution.py:131
  154.3 1.0 collective-permute-start.14
  155.2 0.9 collective-permute-start.13
  156.2 3.3 %collective-permute-start.28 = (f32[96,768]{1,0:T(8,128)S(1)}, f32[96,768]{1,0:T(8,128)S(1)}, u32[]{:S(2)}, u32[]{:S(2)}) collective-permute-start(f32[96,768]{1,0:T(8,128)S(1)} %bitcast_select_fusion), channel_id=1, source_target_pairs={{0,6},{1,7},{2,0},{3,1},{4,2},{5,3},{6,4},{7,5},{8,14},{9,15},{10,... | collective-permute-start | bytes 884744 | tf_op jit(solution)/shard_map/ppermute | solution.py:33
  159.5 2.3 %collective-permute-start.30 = (f32[96,768]{1,0:T(8,128)S(1)}, f32[96,768]{1,0:T(8,128)S(1)}, u32[]{:S(2)}, u32[]{:S(2)}) collective-permute-start(f32[96,768]{1,0:T(8,128)S(1)} %bitcast_select_fusion), channel_id=1, source_target_pairs={{0,2},{1,3},{2,4},{3,5},{4,6},{5,7},{6,0},{7,1},{8,10},{9,11},{10,... | collective-permute-start | bytes 884744 | tf_op jit(solution)/shard_map/ppermute | solution.py:33
  161.8 2.2 %collective-permute-start.16 = (f32[4096]{0:T(1024)S(1)}, f32[4096]{0:T(1024)S(1)}, u32[]{:S(2)}, u32[]{:S(2)}) collective-permute-start(f32[4096]{0:T(1024)S(1)} %maximum_maximum_fusion.1), channel_id=1, source_target_pairs={{0,32},{8,40},{16,48},{24,56},{32,0},{40,8},{48,16},{56,24},{1,33}... | collective-permute-start | bytes 49160 | tf_op jit(solution)/shard_map/ppermute | solution.py:82
  164.1 3.0 %collective-permute-done.16 = f32[4096]{0:T(1024)S(1)} collective-permute-done((f32[4096]{0:T(1024)S(1)}, f32[4096]{0:T(1024)S(1)}, u32[]{:S(2)}, u32[]{:S(2)}) %collective-permute-start.16) | collective-permute-done | bytes 16416 | tf_op jit(solution)/shard_map/ppermute | solution.py:82
  167.2 5.5 %collective-permute-done.29 = f32[96,768]{1,0:T(8,128)S(1)} collective-permute-done((f32[96,768]{1,0:T(8,128)S(1)}, f32[96,768]{1,0:T(8,128)S(1)}, u32[]{:S(2)}, u32[]{:S(2)}) %collective-permute-start.29) | collective-permute-done | bytes 294944 | tf_op jit(solution)/shard_map/ppermute | solution.py:33
  172.7 0.9 collective-permute-done.30
  173.9 10.8 %maximum_reduce_fusion = f32[384]{0:T(512)S(1)} fusion(f32[384,768]{1,0:T(8,128)S(1)} %bitcast.64, f32[4096,768]{1,0:T(8,128)} %all-gather.2.cloned.1.call-done, f32[4096]{0:T(1024)S(1)} %maximum_maximum_fusion), kind=kOutput, calls=%fused_computation.6 | convolution fusion | flops 7252475392 | bytes 13780480 | tf_op jit(solution)/shard_map/dot_general | solution.py:11
  184.8 1.1 collective-permute-start.33
  185.8 3.7 %collective-permute-start.31 = (f32[384]{0:T(512)S(1)}, f32[384]{0:T(512)S(1)}, u32[]{:S(2)}, u32[]{:S(2)}) collective-permute-start(f32[384]{0:T(512)S(1)} %maximum_reduce_fusion), channel_id=1, source_target_pairs={{0,1},{1,0},{2,3},{3,2},{4,5},{5,4},{6,7},{7,6},{8,9},{9,8},{10,11... | collective-permute-start | bytes 4616 | tf_op jit(solution)/shard_map/ppermute | solution.py:47
  189.7 1.5 collective-permute-done.31
  191.8 1.4 collective-permute-start.36
  193.2 3.9 %collective-permute-start.35 = (f32[384]{0:T(512)S(1)}, f32[384]{0:T(512)S(1)}, u32[]{:S(2)}, u32[]{:S(2)}) collective-permute-start(f32[384]{0:T(512)S(1)} %select_reduce_fusion.1), channel_id=1, source_target_pairs={{0,4},{1,5},{2,6},{3,7},{4,0},{5,1},{6,2},{7,3},{8,12},{9,13},{10,... | collective-permute-start | bytes 4616 | tf_op jit(solution)/shard_map/ppermute | solution.py:95
  197.7 0.9 collective-permute-done.35
  198.7 2.0 collective-permute-done.34
  (110 shorter events, 9.4 us)
Async XLA Ops:
  7.2 0.8 copy-start.2
  7.2 2.8 %copy-start.1 = (s32[192]{0:T(256)S(1)}, s32[192]{0:T(256)}, u32[]{:S(2)}) copy-start(s32[192]{0:T(256)} %param.9) | copy-start | bytes 2308
  7.2 72.2 %all-gather.2.cloned.1.call-start = ((), (), s32[]{:S(2)}) async-start(), calls=%async_computation | async-start | bytes 14155776 | tf_op jit(solution)/shard_map/all_gather | solution.py:122
  7.9 3.6 %collective-permute-start = (s32[128]{0:T(128)S(1)}, s32[128]{0:T(128)S(1)}, u32[]{:S(2)}, u32[]{:S(2)}) collective-permute-start(s32[128]{0:T(128)S(1)} %copy-done.2), channel_id=1, source_target_pairs={{0,64},{64,0},{1,65},{65,1},{2,66},{66,2},{3,67},{67,3},{4,68},{68... | collective-permute-start | bytes 1544 | tf_op jit(solution)/shard_map/ppermute | solution.py:125
  9.9 3.6 %collective-permute-start.18 = (s32[192]{0:T(256)S(1)}, s32[192]{0:T(256)S(1)}, u32[]{:S(2)}, u32[]{:S(2)}) collective-permute-start(s32[192]{0:T(256)S(1)} %copy-done.1), channel_id=1, source_target_pairs={{0,64},{64,0},{1,65},{65,1},{2,66},{66,2},{3,67},{67,3},{4,68},{68... | collective-permute-start | bytes 2312 | tf_op jit(solution)/shard_map/ppermute | solution.py:126
  86.3 12.7 %collective-permute-start.3 = (f32[64,768]{1,0:T(8,128)}, f32[64,768]{1,0:T(8,128)S(1)}, u32[]{:S(2)}, u32[]{:S(2)}) collective-permute-start(f32[64,768]{1,0:T(8,128)} %get-tuple-element.9), channel_id=1, source_target_pairs={{0,6},{1,7},{2,0},{3,1},{4,2},{5,3},{6,4},{7,5},{8,14},{9,15},{10,... | collective-permute-start | bytes 589832 | tf_op jit(solution)/shard_map/ppermute | solution.py:33
  86.9 12.2 %collective-permute-start.2 = (f32[64,768]{1,0:T(8,128)}, f32[64,768]{1,0:T(8,128)}, u32[]{:S(2)}, u32[]{:S(2)}) collective-permute-start(f32[64,768]{1,0:T(8,128)} %get-tuple-element.10), channel_id=1, source_target_pairs={{0,4},{1,5},{2,6},{3,7},{4,0},{5,1},{6,2},{7,3},{8,12},{9,13},{10,... | collective-permute-start | bytes 589832 | tf_op jit(solution)/shard_map/ppermute | solution.py:33
  89.3 10.5 %collective-permute-start.1 = (f32[64,768]{1,0:T(8,128)S(1)}, f32[64,768]{1,0:T(8,128)}, u32[]{:S(2)}, u32[]{:S(2)}) collective-permute-start(f32[64,768]{1,0:T(8,128)S(1)} %get-tuple-element.8), channel_id=1, source_target_pairs={{0,2},{1,3},{2,4},{3,5},{4,6},{5,7},{6,0},{7,1},{8,10},{9,11},{10,... | collective-permute-start | bytes 589832 | tf_op jit(solution)/shard_map/ppermute | solution.py:33
  100.8 8.1 %collective-permute-start.6 = (f32[16,768]{1,0:T(8,128)S(1)}, f32[16,768]{1,0:T(8,128)S(1)}, u32[]{:S(2)}, u32[]{:S(2)}) collective-permute-start(f32[16,768]{1,0:T(8,128)S(1)} %get-tuple-element.15), channel_id=1, source_target_pairs={{0,65},{1,64},{2,67},{3,66},{4,69},{5,68},{6,71},{7,70},{64,1},{65... | collective-permute-start | bytes 147464 | tf_op jit(solution)/shard_map/ppermute | solution.py:51
  103.9 12.6 %collective-permute-start.21 = (f32[96,768]{1,0:T(8,128)S(1)}, f32[96,768]{1,0:T(8,128)S(1)}, u32[]{:S(2)}, u32[]{:S(2)}) collective-permute-start(f32[96,768]{1,0:T(8,128)S(1)} %get-tuple-element.6), channel_id=1, source_target_pairs={{0,6},{1,7},{2,0},{3,1},{4,2},{5,3},{6,4},{7,5},{8,14},{9,15},{10,... | collective-permute-start | bytes 884744 | tf_op jit(solution)/shard_map/ppermute | solution.py:33
  106.7 13.1 %collective-permute-start.20 = (f32[96,768]{1,0:T(8,128)S(1)}, f32[96,768]{1,0:T(8,128)S(1)}, u32[]{:S(2)}, u32[]{:S(2)}) collective-permute-start(f32[96,768]{1,0:T(8,128)S(1)} %get-tuple-element.7), channel_id=1, source_target_pairs={{0,4},{1,5},{2,6},{3,7},{4,0},{5,1},{6,2},{7,3},{8,12},{9,13},{10,... | collective-permute-start | bytes 884744 | tf_op jit(solution)/shard_map/ppermute | solution.py:33
  106.9 13.7 %collective-permute-start.19 = (f32[96,768]{1,0:T(8,128)S(1)}, f32[96,768]{1,0:T(8,128)S(1)}, u32[]{:S(2)}, u32[]{:S(2)}) collective-permute-start(f32[96,768]{1,0:T(8,128)S(1)} %get-tuple-element.5), channel_id=1, source_target_pairs={{0,2},{1,3},{2,4},{3,5},{4,6},{5,7},{6,0},{7,1},{8,10},{9,11},{10,... | collective-permute-start | bytes 884744 | tf_op jit(solution)/shard_map/ppermute | solution.py:33
  108.8 4.1 %collective-permute-start.5 = (f32[16,768]{1,0:T(8,128)S(1)}, f32[16,768]{1,0:T(8,128)S(1)}, u32[]{:S(2)}, u32[]{:S(2)}) collective-permute-start(f32[16,768]{1,0:T(8,128)S(1)} %get-tuple-element.16), channel_id=1, source_target_pairs={{0,64},{64,0},{1,65},{65,1},{2,66},{66,2},{3,67},{67,3},{4,68},{68... | collective-permute-start | bytes 147464 | tf_op jit(solution)/shard_map/ppermute | solution.py:49
  108.9 5.6 %collective-permute-start.4 = (f32[16,768]{1,0:T(8,128)S(1)}, f32[16,768]{1,0:T(8,128)S(1)}, u32[]{:S(2)}, u32[]{:S(2)}) collective-permute-start(f32[16,768]{1,0:T(8,128)S(1)} %get-tuple-element.14), channel_id=1, source_target_pairs={{0,1},{1,0},{2,3},{3,2},{4,5},{5,4},{6,7},{7,6},{8,9},{9,8},{10,11... | collective-permute-start | bytes 147464 | tf_op jit(solution)/shard_map/ppermute | solution.py:47
  114.5 6.9 %collective-permute-start.9 = (f32[16,768]{1,0:T(8,128)S(1)}, f32[16,768]{1,0:T(8,128)S(1)}, u32[]{:S(2)}, u32[]{:S(2)}) collective-permute-start(f32[16,768]{1,0:T(8,128)S(1)} %add_add_fusion.3), channel_id=1, source_target_pairs={{0,65},{1,64},{2,67},{3,66},{4,69},{5,68},{6,71},{7,70},{64,1},{65... | collective-permute-start | bytes 147464 | tf_op jit(solution)/shard_map/ppermute | solution.py:51
  116.1 9.3 %collective-permute-start.8 = (f32[16,768]{1,0:T(8,128)S(1)}, f32[16,768]{1,0:T(8,128)S(1)}, u32[]{:S(2)}, u32[]{:S(2)}) collective-permute-start(f32[16,768]{1,0:T(8,128)S(1)} %add_add_fusion.3), channel_id=1, source_target_pairs={{0,64},{64,0},{1,65},{65,1},{2,66},{66,2},{3,67},{67,3},{4,68},{68... | collective-permute-start | bytes 147464 | tf_op jit(solution)/shard_map/ppermute | solution.py:49
  116.6 8.9 %collective-permute-start.7 = (f32[16,768]{1,0:T(8,128)S(1)}, f32[16,768]{1,0:T(8,128)S(1)}, u32[]{:S(2)}, u32[]{:S(2)}) collective-permute-start(f32[16,768]{1,0:T(8,128)S(1)} %add_add_fusion.3), channel_id=1, source_target_pairs={{0,1},{1,0},{2,3},{3,2},{4,5},{5,4},{6,7},{7,6},{8,9},{9,8},{10,11... | collective-permute-start | bytes 147464 | tf_op jit(solution)/shard_map/ppermute | solution.py:47
  120.7 8.4 %collective-permute-start.24 = (f32[24,768]{1,0:T(8,128)S(1)}, f32[24,768]{1,0:T(8,128)S(1)}, u32[]{:S(2)}, u32[]{:S(2)}) collective-permute-start(f32[24,768]{1,0:T(8,128)S(1)} %get-tuple-element.12), channel_id=1, source_target_pairs={{0,65},{1,64},{2,67},{3,66},{4,69},{5,68},{6,71},{7,70},{64,1},{65... | collective-permute-start | bytes 221192 | tf_op jit(solution)/shard_map/ppermute | solution.py:51
  121.1 8.0 %collective-permute-start.23 = (f32[24,768]{1,0:T(8,128)S(1)}, f32[24,768]{1,0:T(8,128)S(1)}, u32[]{:S(2)}, u32[]{:S(2)}) collective-permute-start(f32[24,768]{1,0:T(8,128)S(1)} %get-tuple-element.13), channel_id=1, source_target_pairs={{0,64},{64,0},{1,65},{65,1},{2,66},{66,2},{3,67},{67,3},{4,68},{68... | collective-permute-start | bytes 221192 | tf_op jit(solution)/shard_map/ppermute | solution.py:49
  121.4 7.7 %collective-permute-start.22 = (f32[24,768]{1,0:T(8,128)S(1)}, f32[24,768]{1,0:T(8,128)S(1)}, u32[]{:S(2)}, u32[]{:S(2)}) collective-permute-start(f32[24,768]{1,0:T(8,128)S(1)} %get-tuple-element.11), channel_id=1, source_target_pairs={{0,1},{1,0},{2,3},{3,2},{4,5},{5,4},{6,7},{7,6},{8,9},{9,8},{10,11... | collective-permute-start | bytes 221192 | tf_op jit(solution)/shard_map/ppermute | solution.py:47
  126.1 11.7 %collective-permute-start.10 = (f32[64,768]{1,0:T(8,128)S(1)}, f32[64,768]{1,0:T(8,128)S(1)}, u32[]{:S(2)}, u32[]{:S(2)}) collective-permute-start(f32[64,768]{1,0:T(8,128)S(1)} %bitcast_select_fusion.2), channel_id=1, source_target_pairs={{0,6},{1,7},{2,0},{3,1},{4,2},{5,3},{6,4},{7,5},{8,14},{9,15},{10,... | collective-permute-start | bytes 589832 | tf_op jit(solution)/shard_map/ppermute | solution.py:33
  128.9 9.0 %collective-permute-start.11 = (f32[64,768]{1,0:T(8,128)S(1)}, f32[64,768]{1,0:T(8,128)S(1)}, u32[]{:S(2)}, u32[]{:S(2)}) collective-permute-start(f32[64,768]{1,0:T(8,128)S(1)} %bitcast_select_fusion.2), channel_id=1, source_target_pairs={{0,4},{1,5},{2,6},{3,7},{4,0},{5,1},{6,2},{7,3},{8,12},{9,13},{10,... | collective-permute-start | bytes 589832 | tf_op jit(solution)/shard_map/ppermute | solution.py:33
  129.1 6.1 %collective-permute-start.27 = (f32[24,768]{1,0:T(8,128)S(1)}, f32[24,768]{1,0:T(8,128)S(1)}, u32[]{:S(2)}, u32[]{:S(2)}) collective-permute-start(f32[24,768]{1,0:T(8,128)S(1)} %add_add_fusion.2), channel_id=1, source_target_pairs={{0,65},{1,64},{2,67},{3,66},{4,69},{5,68},{6,71},{7,70},{64,1},{65... | collective-permute-start | bytes 221192 | tf_op jit(solution)/shard_map/ppermute | solution.py:51
  130.1 7.0 %collective-permute-start.26 = (f32[24,768]{1,0:T(8,128)S(1)}, f32[24,768]{1,0:T(8,128)S(1)}, u32[]{:S(2)}, u32[]{:S(2)}) collective-permute-start(f32[24,768]{1,0:T(8,128)S(1)} %add_add_fusion.2), channel_id=1, source_target_pairs={{0,64},{64,0},{1,65},{65,1},{2,66},{66,2},{3,67},{67,3},{4,68},{68... | collective-permute-start | bytes 221192 | tf_op jit(solution)/shard_map/ppermute | solution.py:49
  131.4 5.9 %collective-permute-start.25 = (f32[24,768]{1,0:T(8,128)S(1)}, f32[24,768]{1,0:T(8,128)S(1)}, u32[]{:S(2)}, u32[]{:S(2)}) collective-permute-start(f32[24,768]{1,0:T(8,128)S(1)} %add_add_fusion.2), channel_id=1, source_target_pairs={{0,1},{1,0},{2,3},{3,2},{4,5},{5,4},{6,7},{7,6},{8,9},{9,8},{10,11... | collective-permute-start | bytes 221192 | tf_op jit(solution)/shard_map/ppermute | solution.py:47
  135.3 6.0 %collective-permute-start.12 = (f32[64,768]{1,0:T(8,128)S(1)}, f32[64,768]{1,0:T(8,128)S(1)}, u32[]{:S(2)}, u32[]{:S(2)}) collective-permute-start(f32[64,768]{1,0:T(8,128)S(1)} %bitcast_select_fusion.2), channel_id=1, source_target_pairs={{0,2},{1,3},{2,4},{3,5},{4,6},{5,7},{6,0},{7,1},{8,10},{9,11},{10,... | collective-permute-start | bytes 589832 | tf_op jit(solution)/shard_map/ppermute | solution.py:33
  151.8 15.4 %copy-start = (f32[8192]{0:T(1024)S(1)}, f32[8192]{0:T(1024)}, u32[]{:S(2)}) copy-start(f32[8192]{0:T(1024)} %param.7) | copy-start | bytes 98308
  154.2 5.3 %collective-permute-start.15 = (f32[4096]{0:T(1024)S(1)}, f32[4096]{0:T(1024)S(1)}, u32[]{:S(2)}, u32[]{:S(2)}) collective-permute-start(f32[4096]{0:T(1024)S(1)} %reduce_max.9), channel_id=1, source_target_pairs={{0,24},{8,16},{16,8},{24,0},{32,56},{40,48},{48,40},{56,32},{1,25}... | collective-permute-start | bytes 49160 | tf_op jit(solution)/shard_map/ppermute | solution.py:82
  154.3 7.6 %collective-permute-start.14 = (f32[4096]{0:T(1024)S(1)}, f32[4096]{0:T(1024)S(1)}, u32[]{:S(2)}, u32[]{:S(2)}) collective-permute-start(f32[4096]{0:T(1024)S(1)} %reduce_max.9), channel_id=1, source_target_pairs={{0,16},{8,24},{16,0},{24,8},{32,48},{40,56},{48,32},{56,40},{1,17}... | collective-permute-start | bytes 49160 | tf_op jit(solution)/shard_map/ppermute | solution.py:82
  155.2 6.6 %collective-permute-start.13 = (f32[4096]{0:T(1024)S(1)}, f32[4096]{0:T(1024)S(1)}, u32[]{:S(2)}, u32[]{:S(2)}) collective-permute-start(f32[4096]{0:T(1024)S(1)} %reduce_max.9), channel_id=1, source_target_pairs={{0,8},{8,0},{16,24},{24,16},{32,40},{40,32},{48,56},{56,48},{1,9},... | collective-permute-start | bytes 49160 | tf_op jit(solution)/shard_map/ppermute | solution.py:82
  156.2 11.0 %collective-permute-start.28 = (f32[96,768]{1,0:T(8,128)S(1)}, f32[96,768]{1,0:T(8,128)S(1)}, u32[]{:S(2)}, u32[]{:S(2)}) collective-permute-start(f32[96,768]{1,0:T(8,128)S(1)} %bitcast_select_fusion), channel_id=1, source_target_pairs={{0,6},{1,7},{2,0},{3,1},{4,2},{5,3},{6,4},{7,5},{8,14},{9,15},{10,... | collective-permute-start | bytes 884744 | tf_op jit(solution)/shard_map/ppermute | solution.py:33
  159.5 13.2 %collective-permute-start.29 = (f32[96,768]{1,0:T(8,128)S(1)}, f32[96,768]{1,0:T(8,128)S(1)}, u32[]{:S(2)}, u32[]{:S(2)}) collective-permute-start(f32[96,768]{1,0:T(8,128)S(1)} %bitcast_select_fusion), channel_id=1, source_target_pairs={{0,4},{1,5},{2,6},{3,7},{4,0},{5,1},{6,2},{7,3},{8,12},{9,13},{10,... | collective-permute-start | bytes 884744 | tf_op jit(solution)/shard_map/ppermute | solution.py:33
  159.5 14.1 %collective-permute-start.30 = (f32[96,768]{1,0:T(8,128)S(1)}, f32[96,768]{1,0:T(8,128)S(1)}, u32[]{:S(2)}, u32[]{:S(2)}) collective-permute-start(f32[96,768]{1,0:T(8,128)S(1)} %bitcast_select_fusion), channel_id=1, source_target_pairs={{0,2},{1,3},{2,4},{3,5},{4,6},{5,7},{6,0},{7,1},{8,10},{9,11},{10,... | collective-permute-start | bytes 884744 | tf_op jit(solution)/shard_map/ppermute | solution.py:33
  161.8 5.3 %collective-permute-start.16 = (f32[4096]{0:T(1024)S(1)}, f32[4096]{0:T(1024)S(1)}, u32[]{:S(2)}, u32[]{:S(2)}) collective-permute-start(f32[4096]{0:T(1024)S(1)} %maximum_maximum_fusion.1), channel_id=1, source_target_pairs={{0,32},{8,40},{16,48},{24,56},{32,0},{40,8},{48,16},{56,24},{1,33}... | collective-permute-start | bytes 49160 | tf_op jit(solution)/shard_map/ppermute | solution.py:82
  184.8 4.9 %collective-permute-start.33 = (f32[384]{0:T(512)S(1)}, f32[384]{0:T(512)S(1)}, u32[]{:S(2)}, u32[]{:S(2)}) collective-permute-start(f32[384]{0:T(512)S(1)} %maximum_reduce_fusion), channel_id=1, source_target_pairs={{0,65},{1,64},{2,67},{3,66},{4,69},{5,68},{6,71},{7,70},{64,1},{65... | collective-permute-start | bytes 4616 | tf_op jit(solution)/shard_map/ppermute | solution.py:51
  185.8 3.8 %collective-permute-start.32 = (f32[384]{0:T(512)S(1)}, f32[384]{0:T(512)S(1)}, u32[]{:S(2)}, u32[]{:S(2)}) collective-permute-start(f32[384]{0:T(512)S(1)} %maximum_reduce_fusion), channel_id=1, source_target_pairs={{0,64},{64,0},{1,65},{65,1},{2,66},{66,2},{3,67},{67,3},{4,68},{68... | collective-permute-start | bytes 4616 | tf_op jit(solution)/shard_map/ppermute | solution.py:49
  185.8 5.3 %collective-permute-start.31 = (f32[384]{0:T(512)S(1)}, f32[384]{0:T(512)S(1)}, u32[]{:S(2)}, u32[]{:S(2)}) collective-permute-start(f32[384]{0:T(512)S(1)} %maximum_reduce_fusion), channel_id=1, source_target_pairs={{0,1},{1,0},{2,3},{3,2},{4,5},{5,4},{6,7},{7,6},{8,9},{9,8},{10,11... | collective-permute-start | bytes 4616 | tf_op jit(solution)/shard_map/ppermute | solution.py:47
  189.6 7.5 %collective-permute-start.17 = (f32[4096]{0:T(1024)S(1)}, f32[4096]{0:T(1024)S(1)}, u32[]{:S(2)}, u32[]{:S(2)}) collective-permute-start(f32[4096]{0:T(1024)S(1)} %maximum_maximum_fusion), channel_id=1, source_target_pairs={{0,64},{64,0},{1,65},{65,1},{2,66},{66,2},{3,67},{67,3},{4,68},{68... | collective-permute-start | bytes 49160 | tf_op jit(solution)/shard_map/ppermute | solution.py:137
  191.8 5.9 %collective-permute-start.36 = (f32[384]{0:T(512)S(1)}, f32[384]{0:T(512)S(1)}, u32[]{:S(2)}, u32[]{:S(2)}) collective-permute-start(f32[384]{0:T(512)S(1)} %select_reduce_fusion.1), channel_id=1, source_target_pairs={{0,6},{1,7},{2,4},{3,5},{4,2},{5,3},{6,0},{7,1},{8,14},{9,15},{10,... | collective-permute-start | bytes 4616 | tf_op jit(solution)/shard_map/ppermute | solution.py:95
  193.2 5.4 %collective-permute-start.35 = (f32[384]{0:T(512)S(1)}, f32[384]{0:T(512)S(1)}, u32[]{:S(2)}, u32[]{:S(2)}) collective-permute-start(f32[384]{0:T(512)S(1)} %select_reduce_fusion.1), channel_id=1, source_target_pairs={{0,4},{1,5},{2,6},{3,7},{4,0},{5,1},{6,2},{7,3},{8,12},{9,13},{10,... | collective-permute-start | bytes 4616 | tf_op jit(solution)/shard_map/ppermute | solution.py:95
  197.1 3.6 %collective-permute-start.34 = (f32[384]{0:T(512)S(1)}, f32[384]{0:T(512)S(1)}, u32[]{:S(2)}, u32[]{:S(2)}) collective-permute-start(f32[384]{0:T(512)S(1)} %select_reduce_fusion.1), channel_id=1, source_target_pairs={{0,2},{1,3},{2,0},{3,1},{4,6},{5,7},{6,4},{7,5},{8,10},{9,11},{10,... | collective-permute-start | bytes 4616 | tf_op jit(solution)/shard_map/ppermute | solution.py:95
Sparse Core Ops, SparseCore 0:
  9.7 69.5 all-gather.1
where the time goes:
time: 209 us
  waiting for transfers between devices  93.4 us (45%)
  starting transfers between devices  55.4 us (27%)
  matrix products  21.1 us (10%)
  local copies, waits for them, and re-layouts  17.6 us (8%)
  between operations  14.5 us (7%)
  other arithmetic  6.73 us (3%)
    all_gather x1, waiting for transfers between devices, body(): half = lax.all_gather(slab_embed, 'xc', axis=0, tiled=True)  65.1 us
    dot_general x2, matrix products, similar(): lax.dot_general(left, right, (((1,), (1,)), ((), ())), precision=lax.Prec...  21.1 us
    ppermute x12, starting transfers between devices, y_shift(): return lax.ppermute(value, 'col', pairs)  20 us
    ppermute x5, starting transfers between devices, z_group_shift(): return lax.ppermute(value, 'col', [(c, c ^ 1) for c in range(N_Y * N_Z)])  14.6 us
    gather x2, local copies, waits for them, and re-layouts, lookup(): jnp.take(source, jnp.clip(position, 0, source.shape[0] - 1), axis=0)  13 us
    ppermute x12, waiting for transfers between devices, y_shift(): return lax.ppermute(value, 'col', pairs)  11.7 us
    ppermute x5, starting transfers between devices, z_group_shift(): lax.ppermute(value, ('zl', 'col'), [(i, i ^ N_Y * N_Z ^ 1) for i in range...  7.06 us
    ppermute x3, starting transfers between devices, group_sum_in_order(): lax.ppermute(z_sum, 'col', pairs)  5.3 us
  transfers between devices with their start and end apart: 38, of which 18 were waited for; matrix products, arithmetic and copies ran while one was open for 6% of the time, Pallas kernels for 0%

commit v1 on v0

--- a/solution.py
+++ b/solution.py
@@ -119,7 +119,9 @@
     n_xc = 8
     col_id = lax.axis_index("col")
     zl = lax.axis_index("zl")
-    half = lax.all_gather(slab_embed, "xc", axis=0, tiled=True)
+    half = jnp.concatenate(
+        lax.all_to_all(jnp.stack([slab_embed] * lax.axis_size("xc")), "xc", 0, 0), axis=0
+    )
     first_row = (col_id * 2 + zl) * half.shape[0]
     zl_swap = [(0, 1), (1, 0)]
     both_sel = pair_join(sel_index, lax.ppermute(sel_index, "zl", zl_swap), zl == 0)

time: 209 us -> 276 us (1.32)
  waiting for transfers between devices: 93.4 us -> 161 us
  between operations: 14.5 us -> 1.11 us
  local copies, waits for them, and re-layouts: 17.6 us -> 24.6 us
  starting transfers between devices: 55.4 us -> 60.8 us
    all_to_all x0 -> x1, waiting for transfers between devices: none -> 133 us  [body(): lax.all_to_all(jnp.stack([slab_embed] * lax.axis_size('xc')), 'xc', 0, 0)]
    all_gather x1 -> x0, waiting for transfers between devices: 65.1 us -> none  [body(): half = lax.all_gather(slab_embed, 'xc', axis=0, tiled=True)]
    another operation x0 -> x1, local copies, waits for them, and re-layouts: none -> 7.01 us  [body(): jnp.stack([slab_embed] * lax.axis_size('xc'))]
    all_to_all x0 -> x1, starting transfers between devices: none -> 5.5 us  [body(): lax.all_to_all(jnp.stack([slab_embed] * lax.axis_size('xc')), 'xc', 0, 0)]
  transfers between devices with their start and end apart: 38 -> 38, of which waited for: 18 -> 17; matrix products, arithmetic and copies ran while one was open for 6% -> 4% of each run, Pallas kernels for 0% -> 0%
where the time goes in v1:
time: 276 us
  waiting for transfers between devices  161 us (58%)
  starting transfers between devices  60.8 us (22%)
  local copies, waits for them, and re-layouts  24.6 us (9%)
  matrix products  21.1 us (8%)
  other arithmetic  6.74 us (2%)
    all_to_all x1, waiting for transfers between devices, body(): lax.all_to_all(jnp.stack([slab_embed] * lax.axis_size('xc')), 'xc', 0, 0)  133 us
    dot_general x2, matrix products, similar(): lax.dot_general(left, right, (((1,), (1,)), ((), ())), precision=lax.Prec...  21.1 us
    ppermute x12, starting transfers between devices, y_shift(): return lax.ppermute(value, 'col', pairs)  20.2 us
    ppermute x5, starting transfers between devices, z_group_shift(): return lax.ppermute(value, 'col', [(c, c ^ 1) for c in range(N_Y * N_Z)])  14.5 us
    gather x2, local copies, waits for them, and re-layouts, lookup(): jnp.take(source, jnp.clip(position, 0, source.shape[0] - 1), axis=0)  13 us
    ppermute x12, waiting for transfers between devices, y_shift(): return lax.ppermute(value, 'col', pairs)  10.8 us
    ppermute x5, starting transfers between devices, z_group_shift(): lax.ppermute(value, ('zl', 'col'), [(i, i ^ N_Y * N_Z ^ 1) for i in range...  8.57 us
    another operation x1, local copies, waits for them, and re-layouts, body(): jnp.stack([slab_embed] * lax.axis_size('xc'))  7.01 us
  transfers between devices with their start and end apart: 38, of which 17 were waited for; matrix products, arithmetic and copies ran while one was open for 4% of the time, Pallas kernels for 0%

profile of v1, /device:TPU:8, one launch (start us, length us, event | category | flops | bytes accessed | tf_op | source)
XLA Modules:
  0.0 275.7 jit_solution(2479520542983121587)
XLA Ops:
  0.6 7.0 %stack.91 = f32[8,512,768]{2,1,0:T(8,128)} broadcast(f32[512,768]{1,0:T(8,128)} %param.6), dimensions={1,2} | broadcast | bytes 14155776 | tf_op jit(solution)/shard_map/stack | solution.py:123
  7.6 5.5 %all-to-all-start = ((f32[8,512,768]{2,1,0:T(8,128)}), f32[8,512,768]{2,1,0:T(8,128)}, u32[]{:S(2)}, u32[]{:S(2)}) async-start(f32[8,512,768]{2,1,0:T(8,128)} %stack.91), calls=%async_computation | async-start | bytes 25165824 | tf_op jit(solution)/shard_map/all_to_all | solution.py:123
  13.2 2.0 collective-permute-start
  15.4 1.4 collective-permute-done
  16.8 1.9 collective-permute-done.18
  19.5 133.2 %all-to-all-done = f32[8,512,768]{2,1,0:T(8,128)} async-done(((f32[8,512,768]{2,1,0:T(8,128)}), f32[8,512,768]{2,1,0:T(8,128)}, u32[]{:S(2)}, u32[]{:S(2)}) %all-to-all-start) | async-done | bytes 12582944 | tf_op jit(solution)/shard_map/all_to_all | solution.py:123
  152.7 6.0 %gather_fusion = f32[256,768]{1,0:T(8,128)S(1)} fusion(f32[4096,768]{1,0:T(8,128)} %bitcast, s32[1024]{0:T(1024)S(1)} %pad_clamp_fusion.4), kind=kCustom, calls=%fused_computation.2 | custom fusion | bytes 1573888 | tf_op jit(solution)/shard_map/jit(_take)/gather | solution.py:23
  158.8 0.8 constant_dynamic-slice_fusion.13
  160.1 2.7 collective-permute-start.2
  162.7 1.9 collective-permute-start.1
  164.6 7.1 %gather_fusion.2 = f32[384,768]{1,0:T(8,128)S(1)} fusion(f32[4096,768]{1,0:T(8,128)} %bitcast, s32[1024]{0:T(1024)S(1)} %pad_clamp_fusion.2), kind=kCustom, calls=%fused_computation.4 | custom fusion | bytes 2360832 | tf_op jit(solution)/shard_map/jit(_take)/gather | solution.py:23
  171.7 0.9 select_select_fusion
  172.6 1.1 add_add_fusion.1
  173.7 4.1 %collective-permute-start.6 = (f32[16,768]{1,0:T(8,128)S(1)}, f32[16,768]{1,0:T(8,128)S(1)}, u32[]{:S(2)}, u32[]{:S(2)}) collective-permute-start(f32[16,768]{1,0:T(8,128)S(1)} %get-tuple-element.15), channel_id=1, source_target_pairs={{0,65},{1,64},{2,67},{3,66},{4,69},{5,68},{6,71},{7,70},{64,1},{65... | collective-permute-start | bytes 147464 | tf_op jit(solution)/shard_map/ppermute | solution.py:51
  177.9 2.7 collective-permute-start.21
  180.7 2.0 collective-permute-start.19
  182.8 1.5 collective-permute-start.4
  184.6 2.3 collective-permute-done.5
  186.9 1.5 collective-permute-done.4
  188.4 1.8 collective-permute-start.9
  190.6 2.5 collective-permute-start.7
  193.6 0.7 collective-permute-done.19
  195.1 4.2 %collective-permute-start.22 = (f32[24,768]{1,0:T(8,128)S(1)}, f32[24,768]{1,0:T(8,128)S(1)}, u32[]{:S(2)}, u32[]{:S(2)}) collective-permute-start(f32[24,768]{1,0:T(8,128)S(1)} %get-tuple-element.11), channel_id=1, source_target_pairs={{0,1},{1,0},{2,3},{3,2},{4,5},{5,4},{6,7},{7,6},{8,9},{9,8},{10,11... | collective-permute-start | bytes 221192 | tf_op jit(solution)/shard_map/ppermute | solution.py:47
  199.9 2.7 collective-permute-start.10
  202.9 1.0 collective-permute-start.27
  204.0 1.2 collective-permute-start.26
  205.2 2.5 collective-permute-start.25
  207.8 1.2 collective-permute-done.27
  209.0 1.8 collective-permute-start.12
  211.7 3.3 %collective-permute-done.12 = f32[64,768]{1,0:T(8,128)S(1)} collective-permute-done((f32[64,768]{1,0:T(8,128)S(1)}, f32[64,768]{1,0:T(8,128)S(1)}, u32[]{:S(2)}, u32[]{:S(2)}) %collective-permute-start.12) | collective-permute-done | bytes 196640 | tf_op jit(solution)/shard_map/ppermute | solution.py:33
  215.2 10.3 %fusion.13 = f32[256,4096]{1,0:T(8,128)} fusion(f32[256,768]{1,0:T(8,128)S(1)} %bitcast.62, f32[4096,768]{1,0:T(8,128)} %bitcast), kind=kOutput, calls=%fused_computation.86 | convolution fusion | flops 4831838208 | bytes 17563648 | tf_op jit(solution)/shard_map/dot_general | solution.py:11
  225.5 2.4 reduce_max.9
  228.0 0.7 collective-permute-start.14
  228.6 1.2 collective-permute-start.13
  229.9 3.3 %collective-permute-start.28 = (f32[96,768]{1,0:T(8,128)S(1)}, f32[96,768]{1,0:T(8,128)S(1)}, u32[]{:S(2)}, u32[]{:S(2)}) collective-permute-start(f32[96,768]{1,0:T(8,128)S(1)} %bitcast_select_fusion), channel_id=1, source_target_pairs={{0,6},{1,7},{2,0},{3,1},{4,2},{5,3},{6,4},{7,5},{8,14},{9,15},{10,... | collective-permute-start | bytes 884744 | tf_op jit(solution)/shard_map/ppermute | solution.py:33
  233.2 2.3 collective-permute-start.30
  235.6 1.0 collective-permute-start.16
  236.6 4.3 %collective-permute-done.16 = f32[4096]{0:T(1024)S(1)} collective-permute-done((f32[4096]{0:T(1024)S(1)}, f32[4096]{0:T(1024)S(1)}, u32[]{:S(2)}, u32[]{:S(2)}) %collective-permute-start.16) | collective-permute-done | bytes 16416 | tf_op jit(solution)/shard_map/ppermute | solution.py:82
  240.9 5.5 %collective-permute-done.29 = f32[96,768]{1,0:T(8,128)S(1)} collective-permute-done((f32[96,768]{1,0:T(8,128)S(1)}, f32[96,768]{1,0:T(8,128)S(1)}, u32[]{:S(2)}, u32[]{:S(2)}) %collective-permute-start.29) | collective-permute-done | bytes 294944 | tf_op jit(solution)/shard_map/ppermute | solution.py:33
  246.4 0.9 collective-permute-done.30
  247.6 10.8 %maximum_reduce_fusion = f32[384]{0:T(512)S(1)} fusion(f32[384,768]{1,0:T(8,128)S(1)} %bitcast.65, f32[4096,768]{1,0:T(8,128)} %bitcast, f32[4096]{0:T(1024)S(1)} %maximum_maximum_fusion), kind=kOutput, calls=%fused_computation.6 | convolution fusion | flops 7252475392 | bytes 13780480 | tf_op jit(solution)/shard_map/dot_general | solution.py:11
  258.5 1.1 collective-permute-start.33
  259.6 3.7 %collective-permute-start.31 = (f32[384]{0:T(512)S(1)}, f32[384]{0:T(512)S(1)}, u32[]{:S(2)}, u32[]{:S(2)}) collective-permute-start(f32[384]{0:T(512)S(1)} %maximum_reduce_fusion), channel_id=1, source_target_pairs={{0,1},{1,0},{2,3},{3,2},{4,5},{5,4},{6,7},{7,6},{8,9},{9,8},{10,11... | collective-permute-start | bytes 4616 | tf_op jit(solution)/shard_map/ppermute | solution.py:47
  263.4 1.5 collective-permute-done.31
  265.5 1.4 collective-permute-start.36
  267.0 3.9 %collective-permute-start.35 = (f32[384]{0:T(512)S(1)}, f32[384]{0:T(512)S(1)}, u32[]{:S(2)}, u32[]{:S(2)}) collective-permute-start(f32[384]{0:T(512)S(1)} %select_reduce_fusion.1), channel_id=1, source_target_pairs={{0,4},{1,5},{2,6},{3,7},{4,0},{5,1},{6,2},{7,3},{8,12},{9,13},{10,... | collective-permute-start | bytes 4616 | tf_op jit(solution)/shard_map/ppermute | solution.py:95
  271.5 0.9 collective-permute-done.35
  272.4 2.0 collective-permute-done.34
  (110 shorter events, 9.0 us)
Async XLA Ops:
  7.6 5.5 %copy-start.2 = (s32[128]{0:T(128)S(1)}, s32[128]{0:T(128)}, u32[]{:S(2)}) copy-start(s32[128]{0:T(128)} %param.8) | copy-start | bytes 1540
  7.6 7.5 %copy-start.1 = (s32[192]{0:T(256)S(1)}, s32[192]{0:T(256)}, u32[]{:S(2)}) copy-start(s32[192]{0:T(256)} %param.9) | copy-start | bytes 2308
  7.6 145.1 %all-to-all-start = ((f32[8,512,768]{2,1,0:T(8,128)}), f32[8,512,768]{2,1,0:T(8,128)}, u32[]{:S(2)}, u32[]{:S(2)}) async-start(f32[8,512,768]{2,1,0:T(8,128)} %stack.91), calls=%async_computation | async-start | bytes 25165824 | tf_op jit(solution)/shard_map/all_to_all | solution.py:123
  13.2 3.6 %collective-permute-start = (s32[128]{0:T(128)S(1)}, s32[128]{0:T(128)S(1)}, u32[]{:S(2)}, u32[]{:S(2)}) collective-permute-start(s32[128]{0:T(128)S(1)} %copy-done.2), channel_id=1, source_target_pairs={{0,64},{64,0},{1,65},{65,1},{2,66},{66,2},{3,67},{67,3},{4,68},{68... | collective-permute-start | bytes 1544 | tf_op jit(solution)/shard_map/ppermute | solution.py:127
  15.2 3.6 %collective-permute-start.18 = (s32[192]{0:T(256)S(1)}, s32[192]{0:T(256)S(1)}, u32[]{:S(2)}, u32[]{:S(2)}) collective-permute-start(s32[192]{0:T(256)S(1)} %copy-done.1), channel_id=1, source_target_pairs={{0,64},{64,0},{1,65},{65,1},{2,66},{66,2},{3,67},{67,3},{4,68},{68... | collective-permute-start | bytes 2312 | tf_op jit(solution)/shard_map/ppermute | solution.py:128
  159.7 12.9 %collective-permute-start.3 = (f32[64,768]{1,0:T(8,128)}, f32[64,768]{1,0:T(8,128)S(1)}, u32[]{:S(2)}, u32[]{:S(2)}) collective-permute-start(f32[64,768]{1,0:T(8,128)} %get-tuple-element.9), channel_id=1, source_target_pairs={{0,6},{1,7},{2,0},{3,1},{4,2},{5,3},{6,4},{7,5},{8,14},{9,15},{10,... | collective-permute-start | bytes 589832 | tf_op jit(solution)/shard_map/ppermute | solution.py:33
  160.1 12.5 %collective-permute-start.2 = (f32[64,768]{1,0:T(8,128)}, f32[64,768]{1,0:T(8,128)}, u32[]{:S(2)}, u32[]{:S(2)}) collective-permute-start(f32[64,768]{1,0:T(8,128)} %get-tuple-element.10), channel_id=1, source_target_pairs={{0,4},{1,5},{2,6},{3,7},{4,0},{5,1},{6,2},{7,3},{8,12},{9,13},{10,... | collective-permute-start | bytes 589832 | tf_op jit(solution)/shard_map/ppermute | solution.py:33
  162.7 9.8 %collective-permute-start.1 = (f32[64,768]{1,0:T(8,128)S(1)}, f32[64,768]{1,0:T(8,128)}, u32[]{:S(2)}, u32[]{:S(2)}) collective-permute-start(f32[64,768]{1,0:T(8,128)S(1)} %get-tuple-element.8), channel_id=1, source_target_pairs={{0,2},{1,3},{2,4},{3,5},{4,6},{5,7},{6,0},{7,1},{8,10},{9,11},{10,... | collective-permute-start | bytes 589832 | tf_op jit(solution)/shard_map/ppermute | solution.py:33
  173.7 9.1 %collective-permute-start.6 = (f32[16,768]{1,0:T(8,128)S(1)}, f32[16,768]{1,0:T(8,128)S(1)}, u32[]{:S(2)}, u32[]{:S(2)}) collective-permute-start(f32[16,768]{1,0:T(8,128)S(1)} %get-tuple-element.15), channel_id=1, source_target_pairs={{0,65},{1,64},{2,67},{3,66},{4,69},{5,68},{6,71},{7,70},{64,1},{65... | collective-permute-start | bytes 147464 | tf_op jit(solution)/shard_map/ppermute | solution.py:51
  177.9 12.8 %collective-permute-start.21 = (f32[96,768]{1,0:T(8,128)S(1)}, f32[96,768]{1,0:T(8,128)S(1)}, u32[]{:S(2)}, u32[]{:S(2)}) collective-permute-start(f32[96,768]{1,0:T(8,128)S(1)} %get-tuple-element.6), channel_id=1, source_target_pairs={{0,6},{1,7},{2,0},{3,1},{4,2},{5,3},{6,4},{7,5},{8,14},{9,15},{10,... | collective-permute-start | bytes 884744 | tf_op jit(solution)/shard_map/ppermute | solution.py:33
  180.6 13.1 %collective-permute-start.20 = (f32[96,768]{1,0:T(8,128)S(1)}, f32[96,768]{1,0:T(8,128)S(1)}, u32[]{:S(2)}, u32[]{:S(2)}) collective-permute-start(f32[96,768]{1,0:T(8,128)S(1)} %get-tuple-element.7), channel_id=1, source_target_pairs={{0,4},{1,5},{2,6},{3,7},{4,0},{5,1},{6,2},{7,3},{8,12},{9,13},{10,... | collective-permute-start | bytes 884744 | tf_op jit(solution)/shard_map/ppermute | solution.py:33
  180.7 13.6 %collective-permute-start.19 = (f32[96,768]{1,0:T(8,128)S(1)}, f32[96,768]{1,0:T(8,128)S(1)}, u32[]{:S(2)}, u32[]{:S(2)}) collective-permute-start(f32[96,768]{1,0:T(8,128)S(1)} %get-tuple-element.5), channel_id=1, source_target_pairs={{0,2},{1,3},{2,4},{3,5},{4,6},{5,7},{6,0},{7,1},{8,10},{9,11},{10,... | collective-permute-start | bytes 884744 | tf_op jit(solution)/shard_map/ppermute | solution.py:33
  182.8 4.1 %collective-permute-start.5 = (f32[16,768]{1,0:T(8,128)S(1)}, f32[16,768]{1,0:T(8,128)S(1)}, u32[]{:S(2)}, u32[]{:S(2)}) collective-permute-start(f32[16,768]{1,0:T(8,128)S(1)} %get-tuple-element.16), channel_id=1, source_target_pairs={{0,64},{64,0},{1,65},{65,1},{2,66},{66,2},{3,67},{67,3},{4,68},{68... | collective-permute-start | bytes 147464 | tf_op jit(solution)/shard_map/ppermute | solution.py:49
  182.8 5.6 %collective-permute-start.4 = (f32[16,768]{1,0:T(8,128)S(1)}, f32[16,768]{1,0:T(8,128)S(1)}, u32[]{:S(2)}, u32[]{:S(2)}) collective-permute-start(f32[16,768]{1,0:T(8,128)S(1)} %get-tuple-element.14), channel_id=1, source_target_pairs={{0,1},{1,0},{2,3},{3,2},{4,5},{5,4},{6,7},{7,6},{8,9},{9,8},{10,11... | collective-permute-start | bytes 147464 | tf_op jit(solution)/shard_map/ppermute | solution.py:47
  188.4 6.7 %collective-permute-start.9 = (f32[16,768]{1,0:T(8,128)S(1)}, f32[16,768]{1,0:T(8,128)S(1)}, u32[]{:S(2)}, u32[]{:S(2)}) collective-permute-start(f32[16,768]{1,0:T(8,128)S(1)} %add_add_fusion.3), channel_id=1, source_target_pairs={{0,65},{1,64},{2,67},{3,66},{4,69},{5,68},{6,71},{7,70},{64,1},{65... | collective-permute-start | bytes 147464 | tf_op jit(solution)/shard_map/ppermute | solution.py:51
  190.2 9.1 %collective-permute-start.8 = (f32[16,768]{1,0:T(8,128)S(1)}, f32[16,768]{1,0:T(8,128)S(1)}, u32[]{:S(2)}, u32[]{:S(2)}) collective-permute-start(f32[16,768]{1,0:T(8,128)S(1)} %add_add_fusion.3), channel_id=1, source_target_pairs={{0,64},{64,0},{1,65},{65,1},{2,66},{66,2},{3,67},{67,3},{4,68},{68... | collective-permute-start | bytes 147464 | tf_op jit(solution)/shard_map/ppermute | solution.py:49
  190.6 8.6 %collective-permute-start.7 = (f32[16,768]{1,0:T(8,128)S(1)}, f32[16,768]{1,0:T(8,128)S(1)}, u32[]{:S(2)}, u32[]{:S(2)}) collective-permute-start(f32[16,768]{1,0:T(8,128)S(1)} %add_add_fusion.3), channel_id=1, source_target_pairs={{0,1},{1,0},{2,3},{3,2},{4,5},{5,4},{6,7},{7,6},{8,9},{9,8},{10,11... | collective-permute-start | bytes 147464 | tf_op jit(solution)/shard_map/ppermute | solution.py:47
  194.5 8.4 %collective-permute-start.24 = (f32[24,768]{1,0:T(8,128)S(1)}, f32[24,768]{1,0:T(8,128)S(1)}, u32[]{:S(2)}, u32[]{:S(2)}) collective-permute-start(f32[24,768]{1,0:T(8,128)S(1)} %get-tuple-element.12), channel_id=1, source_target_pairs={{0,65},{1,64},{2,67},{3,66},{4,69},{5,68},{6,71},{7,70},{64,1},{65... | collective-permute-start | bytes 221192 | tf_op jit(solution)/shard_map/ppermute | solution.py:51
  195.1 7.8 %collective-permute-start.23 = (f32[24,768]{1,0:T(8,128)S(1)}, f32[24,768]{1,0:T(8,128)S(1)}, u32[]{:S(2)}, u32[]{:S(2)}) collective-permute-start(f32[24,768]{1,0:T(8,128)S(1)} %get-tuple-element.13), channel_id=1, source_target_pairs={{0,64},{64,0},{1,65},{65,1},{2,66},{66,2},{3,67},{67,3},{4,68},{68... | collective-permute-start | bytes 221192 | tf_op jit(solution)/shard_map/ppermute | solution.py:49
  195.1 7.8 %collective-permute-start.22 = (f32[24,768]{1,0:T(8,128)S(1)}, f32[24,768]{1,0:T(8,128)S(1)}, u32[]{:S(2)}, u32[]{:S(2)}) collective-permute-start(f32[24,768]{1,0:T(8,128)S(1)} %get-tuple-element.11), channel_id=1, source_target_pairs={{0,1},{1,0},{2,3},{3,2},{4,5},{5,4},{6,7},{7,6},{8,9},{9,8},{10,11... | collective-permute-start | bytes 221192 | tf_op jit(solution)/shard_map/ppermute | solution.py:47
  199.9 11.7 %collective-permute-start.10 = (f32[64,768]{1,0:T(8,128)S(1)}, f32[64,768]{1,0:T(8,128)S(1)}, u32[]{:S(2)}, u32[]{:S(2)}) collective-permute-start(f32[64,768]{1,0:T(8,128)S(1)} %bitcast_select_fusion.2), channel_id=1, source_target_pairs={{0,6},{1,7},{2,0},{3,1},{4,2},{5,3},{6,4},{7,5},{8,14},{9,15},{10,... | collective-permute-start | bytes 589832 | tf_op jit(solution)/shard_map/ppermute | solution.py:33
  202.6 9.1 %collective-permute-start.11 = (f32[64,768]{1,0:T(8,128)S(1)}, f32[64,768]{1,0:T(8,128)S(1)}, u32[]{:S(2)}, u32[]{:S(2)}) collective-permute-start(f32[64,768]{1,0:T(8,128)S(1)} %bitcast_select_fusion.2), channel_id=1, source_target_pairs={{0,4},{1,5},{2,6},{3,7},{4,0},{5,1},{6,2},{7,3},{8,12},{9,13},{10,... | collective-permute-start | bytes 589832 | tf_op jit(solution)/shard_map/ppermute | solution.py:33
  202.9 6.1 %collective-permute-start.27 = (f32[24,768]{1,0:T(8,128)S(1)}, f32[24,768]{1,0:T(8,128)S(1)}, u32[]{:S(2)}, u32[]{:S(2)}) collective-permute-start(f32[24,768]{1,0:T(8,128)S(1)} %add_add_fusion.2), channel_id=1, source_target_pairs={{0,65},{1,64},{2,67},{3,66},{4,69},{5,68},{6,71},{7,70},{64,1},{65... | collective-permute-start | bytes 221192 | tf_op jit(solution)/shard_map/ppermute | solution.py:51
  204.0 6.9 %collective-permute-start.26 = (f32[24,768]{1,0:T(8,128)S(1)}, f32[24,768]{1,0:T(8,128)S(1)}, u32[]{:S(2)}, u32[]{:S(2)}) collective-permute-start(f32[24,768]{1,0:T(8,128)S(1)} %add_add_fusion.2), channel_id=1, source_target_pairs={{0,64},{64,0},{1,65},{65,1},{2,66},{66,2},{3,67},{67,3},{4,68},{68... | collective-permute-start | bytes 221192 | tf_op jit(solution)/shard_map/ppermute | solution.py:49
  205.2 5.9 %collective-permute-start.25 = (f32[24,768]{1,0:T(8,128)S(1)}, f32[24,768]{1,0:T(8,128)S(1)}, u32[]{:S(2)}, u32[]{:S(2)}) collective-permute-start(f32[24,768]{1,0:T(8,128)S(1)} %add_add_fusion.2), channel_id=1, source_target_pairs={{0,1},{1,0},{2,3},{3,2},{4,5},{5,4},{6,7},{7,6},{8,9},{9,8},{10,11... | collective-permute-start | bytes 221192 | tf_op jit(solution)/shard_map/ppermute | solution.py:47
  209.0 6.0 %collective-permute-start.12 = (f32[64,768]{1,0:T(8,128)S(1)}, f32[64,768]{1,0:T(8,128)S(1)}, u32[]{:S(2)}, u32[]{:S(2)}) collective-permute-start(f32[64,768]{1,0:T(8,128)S(1)} %bitcast_select_fusion.2), channel_id=1, source_target_pairs={{0,2},{1,3},{2,4},{3,5},{4,6},{5,7},{6,0},{7,1},{8,10},{9,11},{10,... | collective-permute-start | bytes 589832 | tf_op jit(solution)/shard_map/ppermute | solution.py:33
  225.5 15.4 %copy-start = (f32[8192]{0:T(1024)S(1)}, f32[8192]{0:T(1024)}, u32[]{:S(2)}) copy-start(f32[8192]{0:T(1024)} %param.7) | copy-start | bytes 98308
  227.9 5.3 %collective-permute-start.15 = (f32[4096]{0:T(1024)S(1)}, f32[4096]{0:T(1024)S(1)}, u32[]{:S(2)}, u32[]{:S(2)}) collective-permute-start(f32[4096]{0:T(1024)S(1)} %reduce_max.9), channel_id=1, source_target_pairs={{0,24},{8,16},{16,8},{24,0},{32,56},{40,48},{48,40},{56,32},{1,25}... | collective-permute-start | bytes 49160 | tf_op jit(solution)/shard_map/ppermute | solution.py:82
  228.0 7.6 %collective-permute-start.14 = (f32[4096]{0:T(1024)S(1)}, f32[4096]{0:T(1024)S(1)}, u32[]{:S(2)}, u32[]{:S(2)}) collective-permute-start(f32[4096]{0:T(1024)S(1)} %reduce_max.9), channel_id=1, source_target_pairs={{0,16},{8,24},{16,0},{24,8},{32,48},{40,56},{48,32},{56,40},{1,17}... | collective-permute-start | bytes 49160 | tf_op jit(solution)/shard_map/ppermute | solution.py:82
  228.6 6.9 %collective-permute-start.13 = (f32[4096]{0:T(1024)S(1)}, f32[4096]{0:T(1024)S(1)}, u32[]{:S(2)}, u32[]{:S(2)}) collective-permute-start(f32[4096]{0:T(1024)S(1)} %reduce_max.9), channel_id=1, source_target_pairs={{0,8},{8,0},{16,24},{24,16},{32,40},{40,32},{48,56},{56,48},{1,9},... | collective-permute-start | bytes 49160 | tf_op jit(solution)/shard_map/ppermute | solution.py:82
  229.9 11.0 %collective-permute-start.28 = (f32[96,768]{1,0:T(8,128)S(1)}, f32[96,768]{1,0:T(8,128)S(1)}, u32[]{:S(2)}, u32[]{:S(2)}) collective-permute-start(f32[96,768]{1,0:T(8,128)S(1)} %bitcast_select_fusion), channel_id=1, source_target_pairs={{0,6},{1,7},{2,0},{3,1},{4,2},{5,3},{6,4},{7,5},{8,14},{9,15},{10,... | collective-permute-start | bytes 884744 | tf_op jit(solution)/shard_map/ppermute | solution.py:33
  233.2 13.2 %collective-permute-start.29 = (f32[96,768]{1,0:T(8,128)S(1)}, f32[96,768]{1,0:T(8,128)S(1)}, u32[]{:S(2)}, u32[]{:S(2)}) collective-permute-start(f32[96,768]{1,0:T(8,128)S(1)} %bitcast_select_fusion), channel_id=1, source_target_pairs={{0,4},{1,5},{2,6},{3,7},{4,0},{5,1},{6,2},{7,3},{8,12},{9,13},{10,... | collective-permute-start | bytes 884744 | tf_op jit(solution)/shard_map/ppermute | solution.py:33
  233.2 14.1 %collective-permute-start.30 = (f32[96,768]{1,0:T(8,128)S(1)}, f32[96,768]{1,0:T(8,128)S(1)}, u32[]{:S(2)}, u32[]{:S(2)}) collective-permute-start(f32[96,768]{1,0:T(8,128)S(1)} %bitcast_select_fusion), channel_id=1, source_target_pairs={{0,2},{1,3},{2,4},{3,5},{4,6},{5,7},{6,0},{7,1},{8,10},{9,11},{10,... | collective-permute-start | bytes 884744 | tf_op jit(solution)/shard_map/ppermute | solution.py:33
  235.6 5.3 %collective-permute-start.16 = (f32[4096]{0:T(1024)S(1)}, f32[4096]{0:T(1024)S(1)}, u32[]{:S(2)}, u32[]{:S(2)}) collective-permute-start(f32[4096]{0:T(1024)S(1)} %maximum_maximum_fusion.1), channel_id=1, source_target_pairs={{0,32},{8,40},{16,48},{24,56},{32,0},{40,8},{48,16},{56,24},{1,33}... | collective-permute-start | bytes 49160 | tf_op jit(solution)/shard_map/ppermute | solution.py:82
  258.5 4.9 %collective-permute-start.33 = (f32[384]{0:T(512)S(1)}, f32[384]{0:T(512)S(1)}, u32[]{:S(2)}, u32[]{:S(2)}) collective-permute-start(f32[384]{0:T(512)S(1)} %maximum_reduce_fusion), channel_id=1, source_target_pairs={{0,65},{1,64},{2,67},{3,66},{4,69},{5,68},{6,71},{7,70},{64,1},{65... | collective-permute-start | bytes 4616 | tf_op jit(solution)/shard_map/ppermute | solution.py:51
  259.6 3.8 %collective-permute-start.32 = (f32[384]{0:T(512)S(1)}, f32[384]{0:T(512)S(1)}, u32[]{:S(2)}, u32[]{:S(2)}) collective-permute-start(f32[384]{0:T(512)S(1)} %maximum_reduce_fusion), channel_id=1, source_target_pairs={{0,64},{64,0},{1,65},{65,1},{2,66},{66,2},{3,67},{67,3},{4,68},{68... | collective-permute-start | bytes 4616 | tf_op jit(solution)/shard_map/ppermute | solution.py:49
  259.6 5.3 %collective-permute-start.31 = (f32[384]{0:T(512)S(1)}, f32[384]{0:T(512)S(1)}, u32[]{:S(2)}, u32[]{:S(2)}) collective-permute-start(f32[384]{0:T(512)S(1)} %maximum_reduce_fusion), channel_id=1, source_target_pairs={{0,1},{1,0},{2,3},{3,2},{4,5},{5,4},{6,7},{7,6},{8,9},{9,8},{10,11... | collective-permute-start | bytes 4616 | tf_op jit(solution)/shard_map/ppermute | solution.py:47
  263.3 7.6 %collective-permute-start.17 = (f32[4096]{0:T(1024)S(1)}, f32[4096]{0:T(1024)S(1)}, u32[]{:S(2)}, u32[]{:S(2)}) collective-permute-start(f32[4096]{0:T(1024)S(1)} %maximum_maximum_fusion), channel_id=1, source_target_pairs={{0,64},{64,0},{1,65},{65,1},{2,66},{66,2},{3,67},{67,3},{4,68},{68... | collective-permute-start | bytes 49160 | tf_op jit(solution)/shard_map/ppermute | solution.py:139
  265.5 5.9 %collective-permute-start.36 = (f32[384]{0:T(512)S(1)}, f32[384]{0:T(512)S(1)}, u32[]{:S(2)}, u32[]{:S(2)}) collective-permute-start(f32[384]{0:T(512)S(1)} %select_reduce_fusion.1), channel_id=1, source_target_pairs={{0,6},{1,7},{2,4},{3,5},{4,2},{5,3},{6,0},{7,1},{8,14},{9,15},{10,... | collective-permute-start | bytes 4616 | tf_op jit(solution)/shard_map/ppermute | solution.py:95
  267.0 5.4 %collective-permute-start.35 = (f32[384]{0:T(512)S(1)}, f32[384]{0:T(512)S(1)}, u32[]{:S(2)}, u32[]{:S(2)}) collective-permute-start(f32[384]{0:T(512)S(1)} %select_reduce_fusion.1), channel_id=1, source_target_pairs={{0,4},{1,5},{2,6},{3,7},{4,0},{5,1},{6,2},{7,3},{8,12},{9,13},{10,... | collective-permute-start | bytes 4616 | tf_op jit(solution)/shard_map/ppermute | solution.py:95
  270.8 3.6 %collective-permute-start.34 = (f32[384]{0:T(512)S(1)}, f32[384]{0:T(512)S(1)}, u32[]{:S(2)}, u32[]{:S(2)}) collective-permute-start(f32[384]{0:T(512)S(1)} %select_reduce_fusion.1), channel_id=1, source_target_pairs={{0,2},{1,3},{2,0},{3,1},{4,6},{5,7},{6,4},{7,5},{8,10},{9,11},{10,... | collective-permute-start | bytes 4616 | tf_op jit(solution)/shard_map/ppermute | solution.py:95
